TPU v7x, 128 devices: a whole 4x4x4 slice. The times are simulated.
128 devices in a mesh: node: 8 (over x, core), dev: 16 (over z, y).
Axes of the slice: x: 4, y: 4, z: 4, core: 2. Of those that a mesh axis runs over, the one named last changes fastest.
Arguments:
- tokens: bfloat16 [32768, 7168], P(('node', 'dev')), may hold values from -6 to 6
- grad_out: bfloat16 [32768, 7168], P(('node', 'dev')), may hold values from -1.796875 to 1.796875
- router_gates: bfloat16 [32768, 8], P(('node', 'dev')), may hold values from 0.049804688 to 1
- expert_ids: int32 [32768, 8], P(('node', 'dev')), may hold values from 0 to 255, as said below
- slot_plan: int32 [256, 2], replicated, may hold values from 0 to 16, as said below
- w_gate: bfloat16 [8, 7168, 2048], P(None, 'dev', 'node'), may hold values from -0.0625 to 0.0625
- w_up: bfloat16 [8, 7168, 2048], P(None, 'dev', 'node'), may hold values from -0.0625 to 0.0625
- w_down: bfloat16 [8, 2048, 7168], P(None, 'node', 'dev'), may hold values from -0.125 to 0.125
Outputs:
- grad_tokens: bfloat16 [32768, 7168], P(('node', 'dev'))
- grad_gates: float32 [32768, 8], P(('node', 'dev'))
- grad_w_gate: bfloat16 [8, 7168, 2048], P(None, 'dev', 'node')
- grad_w_up: bfloat16 [8, 7168, 2048], P(None, 'dev', 'node')
- grad_w_down: bfloat16 [8, 2048, 7168], P(None, 'node', 'dev')
Inputs may be any that keep to these rules, and one draw needn't show every extreme that they name: `expert_ids`: each token names 8 different experts. Within one block of 256 tokens (the tokens of one device), at most 4 pairs name any one expert that has slots, and in every draw one expert that has slots is named exactly 2 * 2 times in every block. `slot_plan`: exactly 8 rows hold slots: each such row holds two different slots, and every slot 0 .. 15 stands in exactly one row. Every entry of the other rows equals 16.
All inputs are finite; a program needn't handle non-finite values.
Results may differ from a plain program's by a relative error of at most 0.0059.
Values may be sent and summed in bfloat16 or wider, within the bound.
No kernel may reach another device: no remote copies, remote signals or barrier semaphores. Data moves between devices by JAX's collectives and lax.ppermute only.
A program may use at most 128 MiB of HBM per device.

v0:
```python
import jax
import jax.numpy as jnp
from jax import lax
from jax.sharding import PartitionSpec as P

EXPERTS = 256
TOP = 8
CAP = 2


def expert_pass(pieces, slot_gate, slot_up, slot_down):
    x_piece, dy_piece, gate_piece = pieces
    lead_count = x_piece.shape[0]
    slot_count = slot_down.shape[0]
    model_width = x_piece.shape[-1]
    x_rows = x_piece.reshape(-1, model_width)
    dy_split = dy_piece.reshape(-1, slot_count, model_width // slot_count)
    gate_rows = gate_piece.reshape(-1, 1).astype(jnp.float32)
    gate_pre = jnp.dot(x_rows, slot_gate, preferred_element_type=jnp.float32)
    up_pre = jnp.dot(x_rows, slot_up, preferred_element_type=jnp.float32)
    back_proj = jnp.einsum("rsk,shk->rh", dy_split, slot_down, preferred_element_type=jnp.float32)
    sigmoid_gate = jax.nn.sigmoid(gate_pre)
    active = gate_pre * sigmoid_gate
    hidden = active * up_pre
    scaled_back = gate_rows * back_proj
    d_gate = (scaled_back * up_pre * sigmoid_gate * (1.0 + gate_pre * (1.0 - sigmoid_gate))).astype(
        jnp.bfloat16
    )
    d_up = (scaled_back * active).astype(jnp.bfloat16)
    scaled_hidden = (gate_rows * hidden).astype(jnp.bfloat16)
    gate_terms = jnp.sum(back_proj * hidden, axis=-1)
    row_terms = jnp.einsum("rh,dh->rd", d_gate, slot_gate, preferred_element_type=jnp.float32)
    row_terms = row_terms + jnp.einsum(
        "rh,dh->rd", d_up, slot_up, preferred_element_type=jnp.float32
    )
    acc_gate = jnp.einsum("rd,rh->dh", x_rows, d_gate, preferred_element_type=jnp.float32)
    acc_up = jnp.einsum("rd,rh->dh", x_rows, d_up, preferred_element_type=jnp.float32)
    acc_down = jnp.einsum(
        "rsk,rh->shk", dy_split, scaled_hidden, preferred_element_type=jnp.float32
    )
    row_acc = row_terms.reshape(lead_count, slot_count, -1, model_width)
    gate_acc = gate_terms.reshape(lead_count, slot_count, -1)
    return (acc_gate, acc_up, acc_down, row_acc, gate_acc)


def local(tokens, grad_out, router_gates, expert_ids, slot_plan, w_gate, w_up, w_down):
    slot_count = lax.axis_size("dev")
    tok_rows, model_width = tokens.shape
    hidden_width = w_gate.shape[2]
    round_total = w_gate.shape[0]
    pair_total = tok_rows * TOP
    expert_match = expert_ids[:, :, None] == jnp.arange(EXPERTS, dtype=jnp.int32)
    first_slot = jnp.sum(jnp.where(expert_match, slot_plan[:, 0], 0), axis=-1).reshape(pair_total)
    second_slot = jnp.sum(jnp.where(expert_match, slot_plan[:, 1], 0), axis=-1).reshape(pair_total)
    is_live = first_slot < slot_count
    first_hot = (first_slot[:, None] == jnp.arange(slot_count, dtype=jnp.int32)[None, :]).astype(
        jnp.int32
    )
    pair_order = jnp.sum(first_hot * (jnp.cumsum(first_hot, axis=0) - 1), axis=-1)
    pair_slot = jnp.where(pair_order % 2 == 0, first_slot, second_slot)
    target_row = pair_slot * CAP + pair_order // 2
    position_ids = jnp.arange(slot_count * CAP, dtype=jnp.int32)
    chooser = (is_live[None, :] & (target_row[None, :] == position_ids[:, None])).astype(
        jnp.float32
    )
    pick_rows = jnp.sum(chooser.reshape(slot_count * CAP, tok_rows, TOP), axis=-1)
    pick_half = pick_rows.astype(jnp.bfloat16)
    x_send = (
        jnp.dot(pick_half, tokens, preferred_element_type=jnp.float32)
        .astype(jnp.bfloat16)
        .reshape(slot_count, CAP, model_width)
    )
    dy_send = (
        jnp.dot(pick_half, grad_out, preferred_element_type=jnp.float32)
        .astype(jnp.bfloat16)
        .reshape(slot_count, CAP, model_width)
    )
    flat_gates = router_gates.reshape(pair_total).astype(jnp.float32)
    gate_send = (
        jnp.dot(chooser, flat_gates, precision=lax.Precision.HIGHEST)
        .astype(jnp.bfloat16)
        .reshape(slot_count, CAP)
    )
    in_round = (slot_plan[:, 0] < slot_count).astype(jnp.int32)
    expert_rank = jnp.cumsum(in_round) - 1
    holder = jnp.any(slot_plan[:, :, None] == jnp.arange(slot_count, dtype=jnp.int32), axis=1)
    slot_rank = jnp.sum(jnp.where(holder, expert_rank[:, None], 0), axis=0)
    grouping = (slot_rank[None, :] == jnp.arange(round_total, dtype=jnp.int32)[:, None]).astype(
        jnp.bfloat16
    )
    copy_gate = jnp.take(w_gate, slot_rank, axis=0)
    copy_up = jnp.take(w_up, slot_rank, axis=0)
    copy_down = jnp.take(w_down, slot_rank, axis=0)
    slot_gate, slot_up, slot_down = (
        lax.all_to_all(copy_gate, "dev", split_axis=0, concat_axis=0, tiled=True),
        lax.all_to_all(copy_up, "dev", split_axis=0, concat_axis=0, tiled=True),
        lax.all_to_all(copy_down, "dev", split_axis=0, concat_axis=0, tiled=True),
    )
    slot_gate = slot_gate.reshape(model_width, hidden_width)
    slot_up = slot_up.reshape(model_width, hidden_width)
    got_x, got_dy, got_gate = (
        lax.all_to_all(x_send, "dev", split_axis=0, concat_axis=0, tiled=True),
        lax.all_to_all(dy_send, "dev", split_axis=0, concat_axis=0, tiled=True),
        lax.all_to_all(gate_send, "dev", split_axis=0, concat_axis=0, tiled=True),
    )
    totals = expert_pass(
        (
            lax.all_gather(got_x[None], "node", axis=0, tiled=True),
            lax.all_gather(got_dy[None], "node", axis=0, tiled=True),
            lax.all_gather(got_gate[None], "node", axis=0, tiled=True),
        ),
        slot_gate,
        slot_up,
        slot_down,
    )
    acc_gate, acc_up, acc_down, row_acc, gate_acc = totals
    summed_rows, summed_gates = (
        lax.psum_scatter(row_acc, "node", scatter_dimension=0, tiled=True),
        lax.psum_scatter(gate_acc, "node", scatter_dimension=0, tiled=True),
    )
    back_rows, back_gates = (
        lax.all_to_all(summed_rows, "dev", split_axis=1, concat_axis=1, tiled=True),
        lax.all_to_all(summed_gates, "dev", split_axis=1, concat_axis=1, tiled=True),
    )
    grad_tokens = jnp.einsum(
        "qt,qd->td",
        pick_rows,
        back_rows.reshape(slot_count * CAP, model_width),
        precision=lax.Precision.HIGHEST,
    ).astype(jnp.bfloat16)
    grad_gates = jnp.dot(
        back_gates.reshape(slot_count * CAP), chooser, precision=lax.Precision.HIGHEST
    ).reshape(tok_rows, TOP)
    send_gate = acc_gate.astype(jnp.bfloat16).reshape(
        slot_count, model_width // slot_count, hidden_width
    )
    send_up = acc_up.astype(jnp.bfloat16).reshape(
        slot_count, model_width // slot_count, hidden_width
    )
    send_down = acc_down.astype(jnp.bfloat16)
    got_wgate, got_wup, got_wdown = (
        lax.all_to_all(send_gate, "dev", split_axis=0, concat_axis=0, tiled=True),
        lax.all_to_all(send_up, "dev", split_axis=0, concat_axis=0, tiled=True),
        lax.all_to_all(send_down, "dev", split_axis=0, concat_axis=0, tiled=True),
    )
    grad_w_gate = jnp.einsum(
        "js,sdh->jdh", grouping, got_wgate, preferred_element_type=jnp.float32
    ).astype(jnp.bfloat16)
    grad_w_up = jnp.einsum(
        "js,sdh->jdh", grouping, got_wup, preferred_element_type=jnp.float32
    ).astype(jnp.bfloat16)
    grad_w_down = jnp.einsum(
        "js,shk->jhk", grouping, got_wdown, preferred_element_type=jnp.float32
    ).astype(jnp.bfloat16)
    return (grad_tokens, grad_gates, grad_w_gate, grad_w_up, grad_w_down)


def solution(mesh):
    return jax.shard_map(
        local,
        mesh=mesh,
        in_specs=(
            P(("node", "dev"), None),
            P(("node", "dev"), None),
            P(("node", "dev"), None),
            P(("node", "dev"), None),
            P(),
            P(None, "dev", "node"),
            P(None, "dev", "node"),
            P(None, "node", "dev"),
        ),
        out_specs=(
            P(("node", "dev"), None),
            P(("node", "dev"), None),
            P(None, "dev", "node"),
            P(None, "dev", "node"),
            P(None, "node", "dev"),
        ),
        check_vma=False,
    )
```

profile of v0, /device:TPU:14, one launch (start us, length us, event | category | flops | bytes accessed | tf_op | source)
XLA Modules:
  0.0 506.6 jit_solution(3346200505427443808)
XLA Ops:
  8.9 9.2 %select_reduce_fusion = (s32[256,8]{1,0:T(8,128)S(1)}, s32[256,8]{1,0:T(8,128)S(1)}) fusion(s32[256]{0:T(256)S(1)} %bitcast.78, s32[256,8]{1,0:T(8,128)S(1)} %copy.90, s32[256]{0:T(256)S(1)} %bitcast.77), kind=kLoop, calls=%fused_computation.21 | loop fusion | flops 2617344 | bytes 26624 | tf_op jit(solution)/shard_map/reduce_sum | solution.py:54
  27.2 17.7 %all_to_all.60 = bf16[16,2,7168]{2,1,0:T(2,128)(2,1)} all-to-all(bf16[16,2,7168]{2,1,0:T(2,128)(2,1)S(1)} %reshape.235), channel_id=1, replica_groups=mesh['node'=8,'dev'=16] {'dev'}, dimensions={0} | all-to-all | bytes 917504 | tf_op jit(solution)/shard_map/all_to_all | solution.py:102
  62.3 7.3 %all-to-all-start.1 = ((bf16[16,2,7168]{2,1,0:T(2,128)(2,1)}), bf16[16,2,7168]{2,1,0:T(2,128)(2,1)S(1)}, u32[]{:S(2)}, u32[]{:S(2)}) async-start(bf16[16,2,7168]{2,1,0:T(2,128)(2,1)} %reshape.232), calls=%async_computation.1 | async-start | bytes 917504 | tf_op jit(solution)/shard_map/all_to_all | solution.py:103
  85.4 44.8 %all-to-all-done.5 = bf16[16,448,256]{2,1,0:T(8,128)(2,1)} async-done(((bf16[16,448,256]{2,1,0:T(8,128)(2,1)}), bf16[16,448,256]{2,1,0:T(8,128)(2,1)}, u32[]{:S(2)}, u32[]{:S(2)}) %all-to-all-start.5) | async-done | bytes 3670048 | tf_op jit(solution)/shard_map/all_to_all | solution.py:95
  130.2 9.0 %all-to-all-start.4 = ((bf16[16,448,256]{2,1,0:T(8,128)(2,1)}), bf16[16,448,256]{2,1,0:T(8,128)(2,1)}, u32[]{:S(2)}, u32[]{:S(2)}) async-start(bf16[16,448,256]{2,1,0:T(8,128)(2,1)} %get-tuple-element.43), calls=%async_computation.4 | async-start | bytes 7340032 | tf_op jit(solution)/shard_map/all_to_all | solution.py:96
  146.2 38.6 %all-to-all-done.4 = bf16[16,448,256]{2,1,0:T(8,128)(2,1)} async-done(((bf16[16,448,256]{2,1,0:T(8,128)(2,1)}), bf16[16,448,256]{2,1,0:T(8,128)(2,1)}, u32[]{:S(2)}, u32[]{:S(2)}) %all-to-all-start.4) | async-done | bytes 3670048 | tf_op jit(solution)/shard_map/all_to_all | solution.py:96
  184.7 8.8 %all-to-all-start.2 = ((bf16[16,256,448]{1,2,0:T(8,128)(2,1)}), bf16[16,256,448]{1,2,0:T(8,128)(2,1)}, u32[]{:S(2)}, u32[]{:S(2)}) async-start(bf16[16,256,448]{1,2,0:T(8,128)(2,1)} %broadcast_select_fusion.2), calls=%async_computation.2 | async-start | bytes 7340032 | tf_op jit(solution)/shard_map/all_to_all | solution.py:97
  193.6 13.0 %all-gather = bf16[128,1,2]{2,1,0:T(2,128)(2,1)S(1)} all-gather(bf16[16,1,2]{2,1,0:T(2,128)(2,1)S(1)} %all-to-all-done), channel_id=2, replica_groups=mesh['node'=8,'dev'=16] {'node'}, dimensions={0}, use_global_device_ids=true | all-gather | bytes 576 | tf_op jit(solution)/shard_map/all_gather | solution.py:110
  206.9 8.4 %reshape.236 = bf16[256,7168]{1,0:T(8,128)(2,1)} reshape(bf16[128,2,7168]{2,1,0:T(2,128)(2,1)} %all-gather.8.cloned.1.call-done) | data formatting | bytes 7340032 | tf_op jit(solution)/shard_map/reshape | solution.py:16
  215.3 9.6 %reshape.233 = bf16[256,16,448]{2,1,0:T(8,128)(2,1)} reshape(bf16[128,2,7168]{2,1,0:T(2,128)(2,1)} %all-gather.6.cloned.1.call-done) | data formatting | bytes 7340032 | tf_op jit(solution)/shard_map/reshape | solution.py:17
  239.1 8.3 %multiply_reduce_fusion = (f32[256]{0:T(256)S(1)}, bf16[256,256]{0,1:T(8,128)(2,1)S(1)}, bf16[256,256]{0,1:T(8,128)(2,1)S(1)}) fusion(f32[256,256]{0,1:T(8,128)S(1)} %fusion.61, f32[256,256]{0,1:T(8,128)S(1)} %fusion.62, f32[256]{0:T(256)S(1)} %reshape.245, bf16[16,256,448]{1,2,0:T(8,128)(2,1)} %all-to-all-done.2, bf16[256,16,448]{2,1,0:T(8,128)(2,1)} %reshape.233), kind=kOutput, calls=%fused_computation.32 | convolution fusion | flops 940637952 | bytes 8128512 | tf_op jit(solution)/shard_map/rsk,shk->rh/dot_general | solution.py:21
  254.5 8.3 %convolution_add_fusion = f32[256,7168]{1,0:T(8,128)} fusion(f32[256,7168]{1,0:T(8,128)} %fusion.63, bf16[256,256]{0,1:T(8,128)(2,1)S(1)} %get-tuple-element.40, bf16[7168,256]{1,0:T(8,128)(2,1)} %bitcast.9), kind=kOutput, calls=%fused_computation.3 | convolution fusion | flops 941359104 | bytes 18481152 | tf_op jit(solution)/shard_map/rh,dh->rd/dot_general | solution.py:33
  262.8 9.7 %reshape.239 = f32[8,16,2,7168]{3,2,1,0:T(2,128)} reshape(f32[256,7168]{1,0:T(8,128)} %convolution_add_fusion) | data formatting | bytes 14680064 | tf_op jit(solution)/shard_map/reshape | solution.py:41
  272.6 8.3 %copy.96 = f32[8,16,2,7168]{3,1,2,0:T(8,128)} copy(f32[8,16,2,7168]{3,2,1,0:T(2,128)} %reshape.239) | data formatting | bytes 14680064 | tf_op jit(solution)/shard_map/reshape | solution.py:41
  280.9 8.5 %copy.103 = bf16[256,16,448]{0,1,2:T(8,128)(2,1)} copy(bf16[256,16,448]{2,1,0:T(8,128)(2,1)} %reshape.233) | data formatting | bytes 7340032 | tf_op jit(solution)/shard_map/reshape | solution.py:17
  289.4 8.9 %all-to-all-start.7 = ((f32[1,16,2]{2,0,1:T(1,128)}), f32[1,16,2]{2,0,1:T(1,128)S(1)}, u32[]{:S(2)}, u32[]{:S(2)}) async-start(f32[1,16,2]{2,0,1:T(1,128)} %bitcast.76), calls=%async_computation.9 | async-start | bytes 16384 | tf_op jit(solution)/shard_map/all_to_all | solution.py:123
  304.8 7.3 %all-to-all-start.10 = ((bf16[16,256,448]{1,2,0:T(8,128)(2,1)}), bf16[16,256,448]{1,2,0:T(8,128)(2,1)}, u32[]{:S(2)}, u32[]{:S(2)}) async-start(bf16[16,256,448]{1,2,0:T(8,128)(2,1)} %copy.104), calls=%async_computation.12 | async-start | bytes 7340032 | tf_op jit(solution)/shard_map/all_to_all | solution.py:144
  317.2 39.1 %all-to-all-done.10 = bf16[16,256,448]{1,2,0:T(8,128)(2,1)} async-done(((bf16[16,256,448]{1,2,0:T(8,128)(2,1)}), bf16[16,256,448]{1,2,0:T(8,128)(2,1)}, u32[]{:S(2)}, u32[]{:S(2)}) %all-to-all-start.10) | async-done | bytes 3670048 | tf_op jit(solution)/shard_map/all_to_all | solution.py:144
  356.3 8.1 %all-to-all-start.8 = ((bf16[16,448,256]{2,1,0:T(8,128)(2,1)}), bf16[16,448,256]{2,1,0:T(8,128)(2,1)}, u32[]{:S(2)}, u32[]{:S(2)}) async-start(bf16[16,448,256]{2,1,0:T(8,128)(2,1)} %bitcast.72), calls=%async_computation.10 | async-start | bytes 7340032 | tf_op jit(solution)/shard_map/all_to_all | solution.py:142
  369.5 41.6 %all-to-all-done.8 = bf16[16,448,256]{2,1,0:T(8,128)(2,1)} async-done(((bf16[16,448,256]{2,1,0:T(8,128)(2,1)}), bf16[16,448,256]{2,1,0:T(8,128)(2,1)}, u32[]{:S(2)}, u32[]{:S(2)}) %all-to-all-start.8) | async-done | bytes 3670048 | tf_op jit(solution)/shard_map/all_to_all | solution.py:142
  411.0 9.3 %all-to-all-start.9 = ((bf16[16,448,256]{2,1,0:T(8,128)(2,1)}), bf16[16,448,256]{2,1,0:T(8,128)(2,1)}, u32[]{:S(2)}, u32[]{:S(2)}) async-start(bf16[16,448,256]{2,1,0:T(8,128)(2,1)} %bitcast.71), calls=%async_computation.11 | async-start | bytes 7340032 | tf_op jit(solution)/shard_map/all_to_all | solution.py:143
  426.3 38.1 %all-to-all-done.9 = bf16[16,448,256]{2,1,0:T(8,128)(2,1)} async-done(((bf16[16,448,256]{2,1,0:T(8,128)(2,1)}), bf16[16,448,256]{2,1,0:T(8,128)(2,1)}, u32[]{:S(2)}, u32[]{:S(2)}) %all-to-all-start.9) | async-done | bytes 3670048 | tf_op jit(solution)/shard_map/all_to_all | solution.py:143
  464.4 7.9 %all-to-all-start.6 = ((f32[1,16,2,7168]{3,2,0,1:T(2,128)}), f32[1,16,2,7168]{3,2,0,1:T(2,128)S(1)}, u32[]{:S(2)}, u32[]{:S(2)}) async-start(f32[1,16,2,7168]{3,2,0,1:T(2,128)} %copy.97), calls=%async_computation.7 | async-start | bytes 1835008 | tf_op jit(solution)/shard_map/all_to_all | solution.py:122
  491.4 8.5 %convolution_convert_fusion.2 = bf16[256,7168]{1,0:T(8,128)(2,1)} fusion(f32[32,256]{1,0:T(8,128)S(1)} %convert_reduce_fusion, f32[32,7168]{1,0:T(8,128)} %reshape.240), kind=kOutput, calls=%fused_computation.6 | convolution fusion | flops 706478080 | bytes 4620288 | tf_op jit(solution)/shard_map/qt,qd->td/dot_general | solution.py:125
  (101 shorter events, 114.1 us)
Async XLA Ops:
  7.2 44.6 %copy-start = (bf16[8,448,256]{2,1,0:T(8,128)(2,1)S(1)}, bf16[8,448,256]{2,1,0:T(8,128)(2,1)}, u32[]{:S(2)}) copy-start(bf16[8,448,256]{2,1,0:T(8,128)(2,1)} %param.16) | copy-start | bytes 5505028
  7.2 199.7 %all-gather.8.cloned.1.call-start = ((), (), s32[]{:S(2)}) async-start(), calls=%async_computation.16 | async-start | bytes 4128768 | tf_op jit(solution)/shard_map/all_gather | solution.py:108
  23.9 21.2 %copy-start.6 = (bf16[256,8]{0,1:T(8,128)(2,1)S(1)}, bf16[256,8]{0,1:T(8,128)(2,1)}, u32[]{:S(2)}) copy-start(bf16[256,8]{0,1:T(8,128)(2,1)} %param.12) | copy-start | bytes 12292
  24.0 26.9 %copy-start.5 = (s32[256,2]{0,1:T(2,128)S(1)}, s32[256,2]{0,1:T(2,128)}, u32[]{:S(2)}) copy-start(s32[256,2]{0,1:T(2,128)} %param.14) | copy-start | bytes 6148
  46.2 16.1 %all-to-all-start = ((bf16[16,1,2]{2,1,0:T(2,128)(2,1)}), bf16[16,1,2]{2,1,0:T(2,128)(2,1)S(1)}, u32[]{:S(2)}, u32[]{:S(2)}) async-start(bf16[16,1,2]{2,1,0:T(2,128)(2,1)} %all_to_all.48), calls=%async_computation | async-start | bytes 16384 | tf_op jit(solution)/shard_map/all_to_all | solution.py:104
  62.3 15.7 %all-to-all-start.1 = ((bf16[16,2,7168]{2,1,0:T(2,128)(2,1)}), bf16[16,2,7168]{2,1,0:T(2,128)(2,1)S(1)}, u32[]{:S(2)}, u32[]{:S(2)}) async-start(bf16[16,2,7168]{2,1,0:T(2,128)(2,1)} %reshape.232), calls=%async_computation.1 | async-start | bytes 917504 | tf_op jit(solution)/shard_map/all_to_all | solution.py:103
  78.0 0.8 copy-start.4
  78.8 51.4 %all-to-all-start.5 = ((bf16[16,448,256]{2,1,0:T(8,128)(2,1)}), bf16[16,448,256]{2,1,0:T(8,128)(2,1)}, u32[]{:S(2)}, u32[]{:S(2)}) async-start(bf16[16,448,256]{2,1,0:T(8,128)(2,1)} %get-tuple-element.44), calls=%async_computation.5 | async-start | bytes 7340032 | tf_op jit(solution)/shard_map/all_to_all | solution.py:95
  84.6 130.6 %all-gather.6.cloned.1.call-start = ((), (), s32[]{:S(2)}) async-start(), calls=%async_computation.15 | async-start | bytes 4128768 | tf_op jit(solution)/shard_map/all_gather | solution.py:109
  130.2 9.1 %copy-start.3 = (bf16[8,256,448]{1,2,0:T(8,128)(2,1)S(1)}, bf16[8,256,448]{1,2,0:T(8,128)(2,1)}, u32[]{:S(2)}) copy-start(bf16[8,256,448]{1,2,0:T(8,128)(2,1)} %param.17) | copy-start | bytes 5505028
  130.2 54.6 %all-to-all-start.4 = ((bf16[16,448,256]{2,1,0:T(8,128)(2,1)}), bf16[16,448,256]{2,1,0:T(8,128)(2,1)}, u32[]{:S(2)}, u32[]{:S(2)}) async-start(bf16[16,448,256]{2,1,0:T(8,128)(2,1)} %get-tuple-element.43), calls=%async_computation.4 | async-start | bytes 7340032 | tf_op jit(solution)/shard_map/all_to_all | solution.py:96
  184.7 54.4 %all-to-all-start.2 = ((bf16[16,256,448]{1,2,0:T(8,128)(2,1)}), bf16[16,256,448]{1,2,0:T(8,128)(2,1)}, u32[]{:S(2)}, u32[]{:S(2)}) async-start(bf16[16,256,448]{1,2,0:T(8,128)(2,1)} %broadcast_select_fusion.2), calls=%async_computation.2 | async-start | bytes 7340032 | tf_op jit(solution)/shard_map/all_to_all | solution.py:97
  193.5 95.9 %reduce-scatter.5.cloned.1.call-start = ((), (), s32[]{:S(2)}) async-start(), calls=%async_computation.14 | async-start | bytes 73728 | tf_op jit(solution)/shard_map/reduce_scatter | solution.py:119
  224.9 4.8 copy-start.2
  254.4 169.1 %reduce-scatter.3.cloned.1.call-start = ((), (), s32[]{:S(2)}) async-start(), calls=%async_computation.13 | async-start | bytes 8257536 | tf_op jit(solution)/shard_map/reduce_scatter | solution.py:118
  289.4 15.4 %all-to-all-start.7 = ((f32[1,16,2]{2,0,1:T(1,128)}), f32[1,16,2]{2,0,1:T(1,128)S(1)}, u32[]{:S(2)}, u32[]{:S(2)}) async-start(f32[1,16,2]{2,0,1:T(1,128)} %bitcast.76), calls=%async_computation.9 | async-start | bytes 16384 | tf_op jit(solution)/shard_map/all_to_all | solution.py:123
  304.8 51.5 %all-to-all-start.10 = ((bf16[16,256,448]{1,2,0:T(8,128)(2,1)}), bf16[16,256,448]{1,2,0:T(8,128)(2,1)}, u32[]{:S(2)}, u32[]{:S(2)}) async-start(bf16[16,256,448]{1,2,0:T(8,128)(2,1)} %copy.104), calls=%async_computation.12 | async-start | bytes 7340032 | tf_op jit(solution)/shard_map/all_to_all | solution.py:144
  356.3 54.7 %all-to-all-start.8 = ((bf16[16,448,256]{2,1,0:T(8,128)(2,1)}), bf16[16,448,256]{2,1,0:T(8,128)(2,1)}, u32[]{:S(2)}, u32[]{:S(2)}) async-start(bf16[16,448,256]{2,1,0:T(8,128)(2,1)} %bitcast.72), calls=%async_computation.10 | async-start | bytes 7340032 | tf_op jit(solution)/shard_map/all_to_all | solution.py:142
  411.0 53.4 %all-to-all-start.9 = ((bf16[16,448,256]{2,1,0:T(8,128)(2,1)}), bf16[16,448,256]{2,1,0:T(8,128)(2,1)}, u32[]{:S(2)}, u32[]{:S(2)}) async-start(bf16[16,448,256]{2,1,0:T(8,128)(2,1)} %bitcast.71), calls=%async_computation.11 | async-start | bytes 7340032 | tf_op jit(solution)/shard_map/all_to_all | solution.py:143
  464.4 25.4 %all-to-all-start.6 = ((f32[1,16,2,7168]{3,2,0,1:T(2,128)}), f32[1,16,2,7168]{3,2,0,1:T(2,128)S(1)}, u32[]{:S(2)}, u32[]{:S(2)}) async-start(f32[1,16,2,7168]{3,2,0,1:T(2,128)} %copy.97), calls=%async_computation.7 | async-start | bytes 1835008 | tf_op jit(solution)/shard_map/all_to_all | solution.py:122
  488.2 11.7 %copy-start.1 = (bf16[8,448,256]{2,1,0:T(8,128)(2,1)S(1)}, bf16[8,448,256]{2,1,0:T(8,128)(2,1)}, u32[]{:S(2)}) copy-start(bf16[8,448,256]{2,1,0:T(8,128)(2,1)} %param.16) | copy-start | bytes 5505028
Sparse Core Ops, SparseCore 0:
  45.1 26.5 all-gather.7
  87.7 29.2 all-gather.5
  254.6 30.1 reduce-scatter.4
  287.0 47.4 reduce-scatter.2
where the time goes:
time: 516 us; the launch traced here: 507 us
  waiting for transfers between devices  210 us (41%)
  starting transfers between devices  77.3 us (15%)
  local copies, waits for them, and re-layouts  74.5 us (14%)
  matrix products  72.8 us (14%)
  blocking collectives  30.7 us (6%)
  other arithmetic  27.2 us (5%)
  between operations  14.2 us (3%)
    all_to_all x1, waiting for transfers between devices, local(): lax.all_to_all(copy_gate, 'dev', split_axis=0, concat_axis=0, tiled=True)  44.8 us
    all_to_all x1, waiting for transfers between devices, local(): lax.all_to_all(send_gate, 'dev', split_axis=0, concat_axis=0, tiled=True)  41.6 us
    all_to_all x1, waiting for transfers between devices, local(): lax.all_to_all(send_down, 'dev', split_axis=0, concat_axis=0, tiled=True)  39.1 us
    all_to_all x1, waiting for transfers between devices, local(): lax.all_to_all(copy_up, 'dev', split_axis=0, concat_axis=0, tiled=True)  38.6 us
    all_to_all x1, waiting for transfers between devices, local(): lax.all_to_all(send_up, 'dev', split_axis=0, concat_axis=0, tiled=True)  38.1 us
    reshape x2, local copies, waits for them, and re-layouts, expert_pass(): dy_split = dy_piece.reshape(-1, slot_count, model_width // slot_count)  18.1 us
    reshape x2, local copies, waits for them, and re-layouts, expert_pass(): row_acc = row_terms.reshape(lead_count, slot_count, -1, model_width)  18 us
    all_to_all x1, blocking collectives, local(): lax.all_to_all(x_send, 'dev', split_axis=0, concat_axis=0, tiled=True)  17.7 us
  transfers between devices with their start and end apart: 14, of which 7 were waited for; matrix products, arithmetic and copies ran while one was open for 25% of the time, Pallas kernels for 0%

commit v1 on v0

--- a/solution.py
+++ b/solution.py
@@ -107,7 +107,10 @@
         (
             lax.all_gather(got_x[None], "node", axis=0, tiled=True),
             lax.all_gather(got_dy[None], "node", axis=0, tiled=True),
-            lax.all_gather(got_gate[None], "node", axis=0, tiled=True),
+            jnp.concatenate(
+                lax.all_to_all(jnp.stack([got_gate[None]] * lax.axis_size("node")), "node", 0, 0),
+                axis=0,
+            ),
         ),
         slot_gate,
         slot_up,

time: 516 us -> 531 us (1.029)
  waiting for transfers between devices: 210 us -> 233 us
  blocking collectives: 30.7 us -> 17.7 us
    all_gather x1 -> x0, blocking collectives: 13 us -> none  [local(): lax.all_gather(got_gate[None], 'node', axis=0, tiled=True)]
    all_to_all x1, waiting for transfers between devices: 5.71 us -> 17 us  [local(): lax.all_to_all(copy_down, 'dev', split_axis=0, concat_axis=0, tiled=True)]
  transfers between devices with their start and end apart: 14 -> 15, of which waited for: 7 -> 8; matrix products, arithmetic and copies ran while one was open for 25% -> 25% of each run, Pallas kernels for 0% -> 0%
where the time goes in v1:
time: 531 us; the launch traced here: 521 us
  waiting for transfers between devices  233 us (44%)
  starting transfers between devices  81.6 us (15%)
  local copies, waits for them, and re-layouts  75.4 us (14%)
  matrix products  72.9 us (14%)
  other arithmetic  27 us (5%)
  blocking collectives  17.7 us (3%)
  between operations  14.2 us (3%)
    all_to_all x1, waiting for transfers between devices, local(): lax.all_to_all(copy_gate, 'dev', split_axis=0, concat_axis=0, tiled=True)  48.6 us
    all_to_all x1, waiting for transfers between devices, local(): lax.all_to_all(send_down, 'dev', split_axis=0, concat_axis=0, tiled=True)  41.6 us
    all_to_all x1, waiting for transfers between devices, local(): lax.all_to_all(send_up, 'dev', split_axis=0, concat_axis=0, tiled=True)  40.2 us
    all_to_all x1, waiting for transfers between devices, local(): lax.all_to_all(send_gate, 'dev', split_axis=0, concat_axis=0, tiled=True)  39.6 us
    all_to_all x1, waiting for transfers between devices, local(): lax.all_to_all(copy_up, 'dev', split_axis=0, concat_axis=0, tiled=True)  39.2 us
    reshape x2, local copies, waits for them, and re-layouts, expert_pass(): dy_split = dy_piece.reshape(-1, slot_count, model_width // slot_count)  18.1 us
    reshape x2, local copies, waits for them, and re-layouts, expert_pass(): row_acc = row_terms.reshape(lead_count, slot_count, -1, model_width)  18 us
    all_to_all x1, blocking collectives, local(): lax.all_to_all(x_send, 'dev', split_axis=0, concat_axis=0, tiled=True)  17.7 us
  transfers between devices with their start and end apart: 15, of which 8 were waited for; matrix products, arithmetic and copies ran while one was open for 25% of the time, Pallas kernels for 0%

profile of v1, /device:TPU:14, one launch (start us, length us, event | category | flops | bytes accessed | tf_op | source)
XLA Modules:
  0.0 521.3 jit_solution(7929755637342573438)
XLA Ops:
  8.9 9.2 %select_reduce_fusion = (s32[256,8]{1,0:T(8,128)S(1)}, s32[256,8]{1,0:T(8,128)S(1)}) fusion(s32[256]{0:T(256)S(1)} %bitcast.83, s32[256,8]{1,0:T(8,128)S(1)} %copy.79, s32[256]{0:T(256)S(1)} %bitcast.82), kind=kLoop, calls=%fused_computation.21 | loop fusion | flops 2617344 | bytes 26624 | tf_op jit(solution)/shard_map/reduce_sum | solution.py:54
  27.2 17.7 %all_to_all.65 = bf16[16,2,7168]{2,1,0:T(2,128)(2,1)} all-to-all(bf16[16,2,7168]{2,1,0:T(2,128)(2,1)S(1)} %reshape.238), channel_id=1, replica_groups=mesh['node'=8,'dev'=16] {'dev'}, dimensions={0} | all-to-all | bytes 917504 | tf_op jit(solution)/shard_map/all_to_all | solution.py:102
  75.3 7.0 %broadcast_select_fusion.1 = (bf16[16,448,256]{2,1,0:T(8,128)(2,1)}, bf16[16,448,256]{2,1,0:T(8,128)(2,1)}) fusion(bf16[16,448,256]{2,1,0:T(8,128)(2,1)} %gather_fusion.1, pred[16]{0:T(512)(128)(4,1)S(1)} %compare_and_fusion, bf16[16,448,256]{2,1,0:T(8,128)(2,1)} %gather_fusion.2), kind=kLoop, calls=%fused_computation.19 | loop fusion | flops 3670016 | bytes 14680080 | tf_op jit(solution)/shard_map/jit(_take)/select_n | solution.py:92
  92.5 48.6 %all-to-all-done.6 = bf16[16,448,256]{2,1,0:T(8,128)(2,1)} async-done(((bf16[16,448,256]{2,1,0:T(8,128)(2,1)}), bf16[16,448,256]{2,1,0:T(8,128)(2,1)}, u32[]{:S(2)}, u32[]{:S(2)}) %all-to-all-start.6) | async-done | bytes 3670048 | tf_op jit(solution)/shard_map/all_to_all | solution.py:95
  141.1 9.1 %all-to-all-start.5 = ((bf16[16,448,256]{2,1,0:T(8,128)(2,1)}), bf16[16,448,256]{2,1,0:T(8,128)(2,1)}, u32[]{:S(2)}, u32[]{:S(2)}) async-start(bf16[16,448,256]{2,1,0:T(8,128)(2,1)} %get-tuple-element.38), calls=%async_computation.5 | async-start | bytes 7340032 | tf_op jit(solution)/shard_map/all_to_all | solution.py:96
  157.2 39.2 %all-to-all-done.5 = bf16[16,448,256]{2,1,0:T(8,128)(2,1)} async-done(((bf16[16,448,256]{2,1,0:T(8,128)(2,1)}), bf16[16,448,256]{2,1,0:T(8,128)(2,1)}, u32[]{:S(2)}, u32[]{:S(2)}) %all-to-all-start.5) | async-done | bytes 3670048 | tf_op jit(solution)/shard_map/all_to_all | solution.py:96
  196.4 9.6 %all-to-all-start.3 = ((bf16[16,256,448]{1,2,0:T(8,128)(2,1)}), bf16[16,256,448]{1,2,0:T(8,128)(2,1)}, u32[]{:S(2)}, u32[]{:S(2)}) async-start(bf16[16,256,448]{1,2,0:T(8,128)(2,1)} %broadcast_select_fusion.2), calls=%async_computation.3 | async-start | bytes 7340032 | tf_op jit(solution)/shard_map/all_to_all | solution.py:97
  206.6 8.4 %reshape.239 = bf16[256,7168]{1,0:T(8,128)(2,1)} reshape(bf16[128,2,7168]{2,1,0:T(2,128)(2,1)} %all-gather.7.cloned.1.call-done) | data formatting | bytes 7340032 | tf_op jit(solution)/shard_map/reshape | solution.py:16
  215.0 9.6 %reshape.236 = bf16[256,16,448]{2,1,0:T(8,128)(2,1)} reshape(bf16[128,2,7168]{2,1,0:T(2,128)(2,1)} %all-gather.5.cloned.1.call-done) | data formatting | bytes 7340032 | tf_op jit(solution)/shard_map/reshape | solution.py:17
  233.1 17.0 %all-to-all-done.3 = bf16[16,256,448]{1,2,0:T(8,128)(2,1)} async-done(((bf16[16,256,448]{1,2,0:T(8,128)(2,1)}), bf16[16,256,448]{1,2,0:T(8,128)(2,1)}, u32[]{:S(2)}, u32[]{:S(2)}) %all-to-all-start.3) | async-done | bytes 3670048 | tf_op jit(solution)/shard_map/all_to_all | solution.py:97
  250.1 8.3 %multiply_reduce_fusion = (f32[256]{0:T(256)S(1)}, bf16[256,256]{0,1:T(8,128)(2,1)S(1)}, bf16[256,256]{0,1:T(8,128)(2,1)S(1)}) fusion(f32[256,256]{0,1:T(8,128)S(1)} %fusion.61, f32[256,256]{0,1:T(8,128)S(1)} %fusion.62, f32[256]{0:T(256)S(1)} %reshape.248, bf16[16,256,448]{1,2,0:T(8,128)(2,1)} %all-to-all-done.3, bf16[256,16,448]{2,1,0:T(8,128)(2,1)} %reshape.236), kind=kOutput, calls=%fused_computation.32 | convolution fusion | flops 940637952 | bytes 8128512 | tf_op jit(solution)/shard_map/rsk,shk->rh/dot_general | solution.py:21
  265.5 8.4 %convolution_add_fusion = f32[256,7168]{1,0:T(8,128)} fusion(f32[256,7168]{1,0:T(8,128)} %fusion.63, bf16[256,256]{0,1:T(8,128)(2,1)S(1)} %get-tuple-element.35, bf16[7168,256]{1,0:T(8,128)(2,1)} %bitcast.10), kind=kOutput, calls=%fused_computation.3 | convolution fusion | flops 941359104 | bytes 18481152 | tf_op jit(solution)/shard_map/rh,dh->rd/dot_general | solution.py:33
  273.9 9.7 %reshape.242 = f32[8,16,2,7168]{3,2,1,0:T(2,128)} reshape(f32[256,7168]{1,0:T(8,128)} %convolution_add_fusion) | data formatting | bytes 14680064 | tf_op jit(solution)/shard_map/reshape | solution.py:41
  283.6 8.3 %copy.88 = f32[8,16,2,7168]{3,1,2,0:T(8,128)} copy(f32[8,16,2,7168]{3,2,1,0:T(2,128)} %reshape.242) | data formatting | bytes 14680064 | tf_op jit(solution)/shard_map/reshape | solution.py:41
  291.9 8.5 %copy.95 = bf16[256,16,448]{0,1,2:T(8,128)(2,1)} copy(bf16[256,16,448]{2,1,0:T(8,128)(2,1)} %reshape.236) | data formatting | bytes 7340032 | tf_op jit(solution)/shard_map/reshape | solution.py:17
  300.4 7.9 %all-to-all-start.8 = ((f32[1,16,2]{2,0,1:T(1,128)}), f32[1,16,2]{2,0,1:T(1,128)S(1)}, u32[]{:S(2)}, u32[]{:S(2)}) async-start(f32[1,16,2]{2,0,1:T(1,128)} %bitcast.81), calls=%async_computation.10 | async-start | bytes 16384 | tf_op jit(solution)/shard_map/all_to_all | solution.py:126
  314.8 7.3 %all-to-all-start.11 = ((bf16[16,256,448]{1,2,0:T(8,128)(2,1)}), bf16[16,256,448]{1,2,0:T(8,128)(2,1)}, u32[]{:S(2)}, u32[]{:S(2)}) async-start(bf16[16,256,448]{1,2,0:T(8,128)(2,1)} %copy.96), calls=%async_computation.13 | async-start | bytes 7340032 | tf_op jit(solution)/shard_map/all_to_all | solution.py:147
  327.2 41.6 %all-to-all-done.11 = bf16[16,256,448]{1,2,0:T(8,128)(2,1)} async-done(((bf16[16,256,448]{1,2,0:T(8,128)(2,1)}), bf16[16,256,448]{1,2,0:T(8,128)(2,1)}, u32[]{:S(2)}, u32[]{:S(2)}) %all-to-all-start.11) | async-done | bytes 3670048 | tf_op jit(solution)/shard_map/all_to_all | solution.py:147
  368.8 9.9 %all-to-all-start.9 = ((bf16[16,448,256]{2,1,0:T(8,128)(2,1)}), bf16[16,448,256]{2,1,0:T(8,128)(2,1)}, u32[]{:S(2)}, u32[]{:S(2)}) async-start(bf16[16,448,256]{2,1,0:T(8,128)(2,1)} %bitcast.77), calls=%async_computation.11 | async-start | bytes 7340032 | tf_op jit(solution)/shard_map/all_to_all | solution.py:145
  383.8 39.6 %all-to-all-done.9 = bf16[16,448,256]{2,1,0:T(8,128)(2,1)} async-done(((bf16[16,448,256]{2,1,0:T(8,128)(2,1)}), bf16[16,448,256]{2,1,0:T(8,128)(2,1)}, u32[]{:S(2)}, u32[]{:S(2)}) %all-to-all-start.9) | async-done | bytes 3670048 | tf_op jit(solution)/shard_map/all_to_all | solution.py:145
  423.4 8.4 %all-to-all-start.10 = ((bf16[16,448,256]{2,1,0:T(8,128)(2,1)}), bf16[16,448,256]{2,1,0:T(8,128)(2,1)}, u32[]{:S(2)}, u32[]{:S(2)}) async-start(bf16[16,448,256]{2,1,0:T(8,128)(2,1)} %bitcast.76), calls=%async_computation.12 | async-start | bytes 7340032 | tf_op jit(solution)/shard_map/all_to_all | solution.py:146
  437.9 40.2 %all-to-all-done.10 = bf16[16,448,256]{2,1,0:T(8,128)(2,1)} async-done(((bf16[16,448,256]{2,1,0:T(8,128)(2,1)}), bf16[16,448,256]{2,1,0:T(8,128)(2,1)}, u32[]{:S(2)}, u32[]{:S(2)}) %all-to-all-start.10) | async-done | bytes 3670048 | tf_op jit(solution)/shard_map/all_to_all | solution.py:146
  478.0 9.0 %all-to-all-start.7 = ((f32[1,16,2,7168]{3,2,0,1:T(2,128)}), f32[1,16,2,7168]{3,2,0,1:T(2,128)S(1)}, u32[]{:S(2)}, u32[]{:S(2)}) async-start(f32[1,16,2,7168]{3,2,0,1:T(2,128)} %copy.89), calls=%async_computation.8 | async-start | bytes 1835008 | tf_op jit(solution)/shard_map/all_to_all | solution.py:125
  506.0 8.5 %convolution_convert_fusion.2 = bf16[256,7168]{1,0:T(8,128)(2,1)} fusion(f32[32,256]{1,0:T(8,128)S(1)} %convert_reduce_fusion, f32[32,7168]{1,0:T(8,128)} %reshape.243), kind=kOutput, calls=%fused_computation.6 | convolution fusion | flops 706478080 | bytes 4620288 | tf_op jit(solution)/shard_map/qt,qd->td/dot_general | solution.py:128
  (105 shorter events, 116.0 us)
Async XLA Ops:
  7.2 55.5 %copy-start = (bf16[8,448,256]{2,1,0:T(8,128)(2,1)S(1)}, bf16[8,448,256]{2,1,0:T(8,128)(2,1)}, u32[]{:S(2)}) copy-start(bf16[8,448,256]{2,1,0:T(8,128)(2,1)} %param.16) | copy-start | bytes 5505028
  7.2 199.4 %all-gather.7.cloned.1.call-start = ((), (), s32[]{:S(2)}) async-start(), calls=%async_computation.17 | async-start | bytes 4128768 | tf_op jit(solution)/shard_map/all_gather | solution.py:108
  23.9 21.2 %copy-start.6 = (bf16[256,8]{0,1:T(8,128)(2,1)S(1)}, bf16[256,8]{0,1:T(8,128)(2,1)}, u32[]{:S(2)}) copy-start(bf16[256,8]{0,1:T(8,128)(2,1)} %param.12) | copy-start | bytes 12292
  24.0 26.9 %copy-start.5 = (s32[256,2]{0,1:T(2,128)S(1)}, s32[256,2]{0,1:T(2,128)}, u32[]{:S(2)}) copy-start(s32[256,2]{0,1:T(2,128)} %param.14) | copy-start | bytes 6148
  46.2 10.9 %all-to-all-start = ((bf16[16,1,2]{2,1,0:T(2,128)(2,1)}), bf16[16,1,2]{2,1,0:T(2,128)(2,1)S(1)}, u32[]{:S(2)}, u32[]{:S(2)}) async-start(bf16[16,1,2]{2,1,0:T(2,128)(2,1)} %all_to_all.52), calls=%async_computation | async-start | bytes 16384 | tf_op jit(solution)/shard_map/all_to_all | solution.py:104
  57.8 12.6 %all-to-all-start.1 = ((bf16[8,1,16,2]{2,3,1,0:T(2,128)(2,1)}), bf16[8,1,16,2]{2,3,1,0:T(2,128)(2,1)S(1)}, u32[]{:S(2)}, u32[]{:S(2)}) async-start(bf16[8,1,16,2]{2,3,1,0:T(2,128)(2,1)} %stack.3), calls=%async_computation.1 | async-start | bytes 8192 | tf_op jit(solution)/shard_map/all_to_all | solution.py:111
  70.4 14.9 %all-to-all-start.2 = ((bf16[16,2,7168]{2,1,0:T(2,128)(2,1)}), bf16[16,2,7168]{2,1,0:T(2,128)(2,1)S(1)}, u32[]{:S(2)}, u32[]{:S(2)}) async-start(bf16[16,2,7168]{2,1,0:T(2,128)(2,1)} %reshape.235), calls=%async_computation.2 | async-start | bytes 917504 | tf_op jit(solution)/shard_map/all_to_all | solution.py:103
  85.3 0.8 copy-start.4
  86.1 55.1 %all-to-all-start.6 = ((bf16[16,448,256]{2,1,0:T(8,128)(2,1)}), bf16[16,448,256]{2,1,0:T(8,128)(2,1)}, u32[]{:S(2)}, u32[]{:S(2)}) async-start(bf16[16,448,256]{2,1,0:T(8,128)(2,1)} %get-tuple-element.39), calls=%async_computation.6 | async-start | bytes 7340032 | tf_op jit(solution)/shard_map/all_to_all | solution.py:95
  91.8 123.2 %all-gather.5.cloned.1.call-start = ((), (), s32[]{:S(2)}) async-start(), calls=%async_computation.16 | async-start | bytes 4128768 | tf_op jit(solution)/shard_map/all_gather | solution.py:109
  141.1 9.1 %copy-start.3 = (bf16[8,256,448]{1,2,0:T(8,128)(2,1)S(1)}, bf16[8,256,448]{1,2,0:T(8,128)(2,1)}, u32[]{:S(2)}) copy-start(bf16[8,256,448]{1,2,0:T(8,128)(2,1)} %param.17) | copy-start | bytes 5505028
  141.1 55.3 %all-to-all-start.5 = ((bf16[16,448,256]{2,1,0:T(8,128)(2,1)}), bf16[16,448,256]{2,1,0:T(8,128)(2,1)}, u32[]{:S(2)}, u32[]{:S(2)}) async-start(bf16[16,448,256]{2,1,0:T(8,128)(2,1)} %get-tuple-element.38), calls=%async_computation.5 | async-start | bytes 7340032 | tf_op jit(solution)/shard_map/all_to_all | solution.py:96
  196.4 53.7 %all-to-all-start.3 = ((bf16[16,256,448]{1,2,0:T(8,128)(2,1)}), bf16[16,256,448]{1,2,0:T(8,128)(2,1)}, u32[]{:S(2)}, u32[]{:S(2)}) async-start(bf16[16,256,448]{1,2,0:T(8,128)(2,1)} %broadcast_select_fusion.2), calls=%async_computation.3 | async-start | bytes 7340032 | tf_op jit(solution)/shard_map/all_to_all | solution.py:97
  206.1 94.3 %reduce-scatter.5.cloned.1.call-start = ((), (), s32[]{:S(2)}) async-start(), calls=%async_computation.15 | async-start | bytes 73728 | tf_op jit(solution)/shard_map/reduce_scatter | solution.py:122
  224.6 4.8 copy-start.2
  265.5 169.6 %reduce-scatter.3.cloned.1.call-start = ((), (), s32[]{:S(2)}) async-start(), calls=%async_computation.14 | async-start | bytes 8257536 | tf_op jit(solution)/shard_map/reduce_scatter | solution.py:121
  300.4 14.4 %all-to-all-start.8 = ((f32[1,16,2]{2,0,1:T(1,128)}), f32[1,16,2]{2,0,1:T(1,128)S(1)}, u32[]{:S(2)}, u32[]{:S(2)}) async-start(f32[1,16,2]{2,0,1:T(1,128)} %bitcast.81), calls=%async_computation.10 | async-start | bytes 16384 | tf_op jit(solution)/shard_map/all_to_all | solution.py:126
  314.8 54.0 %all-to-all-start.11 = ((bf16[16,256,448]{1,2,0:T(8,128)(2,1)}), bf16[16,256,448]{1,2,0:T(8,128)(2,1)}, u32[]{:S(2)}, u32[]{:S(2)}) async-start(bf16[16,256,448]{1,2,0:T(8,128)(2,1)} %copy.96), calls=%async_computation.13 | async-start | bytes 7340032 | tf_op jit(solution)/shard_map/all_to_all | solution.py:147
  368.8 54.6 %all-to-all-start.9 = ((bf16[16,448,256]{2,1,0:T(8,128)(2,1)}), bf16[16,448,256]{2,1,0:T(8,128)(2,1)}, u32[]{:S(2)}, u32[]{:S(2)}) async-start(bf16[16,448,256]{2,1,0:T(8,128)(2,1)} %bitcast.77), calls=%async_computation.11 | async-start | bytes 7340032 | tf_op jit(solution)/shard_map/all_to_all | solution.py:145
  423.4 54.7 %all-to-all-start.10 = ((bf16[16,448,256]{2,1,0:T(8,128)(2,1)}), bf16[16,448,256]{2,1,0:T(8,128)(2,1)}, u32[]{:S(2)}, u32[]{:S(2)}) async-start(bf16[16,448,256]{2,1,0:T(8,128)(2,1)} %bitcast.76), calls=%async_computation.12 | async-start | bytes 7340032 | tf_op jit(solution)/shard_map/all_to_all | solution.py:146
  478.0 26.4 %all-to-all-start.7 = ((f32[1,16,2,7168]{3,2,0,1:T(2,128)}), f32[1,16,2,7168]{3,2,0,1:T(2,128)S(1)}, u32[]{:S(2)}, u32[]{:S(2)}) async-start(f32[1,16,2,7168]{3,2,0,1:T(2,128)} %copy.89), calls=%async_computation.8 | async-start | bytes 1835008 | tf_op jit(solution)/shard_map/all_to_all | solution.py:125
  502.9 11.7 %copy-start.1 = (bf16[8,448,256]{2,1,0:T(8,128)(2,1)S(1)}, bf16[8,448,256]{2,1,0:T(8,128)(2,1)}, u32[]{:S(2)}) copy-start(bf16[8,448,256]{2,1,0:T(8,128)(2,1)} %param.16) | copy-start | bytes 5505028
Sparse Core Ops, SparseCore 0:
  45.1 26.5 all-gather.6
  94.9 29.2 all-gather.4
  265.6 29.2 reduce-scatter.4
  297.1 47.3 reduce-scatter.2
